TPU v7x, 512 devices: a whole 4x8x8 slice. The times are simulated.
512 devices in a mesh: grp: 32 (over x, y), tp: 16 (over z, core).
Axes of the slice: x: 4, y: 8, z: 8, core: 2. Of those that a mesh axis runs over, the one named last changes fastest.
Arguments:
- patches: bfloat16 [16384, 1664], P('grp'), may hold values from -6 to 6
- patch_image: int32 [16384], P('grp'), may hold values from 0 to 4095, as said below
- vis_gain: float32 [1664], replicated, may hold values from 0.25 to 1.75
- vis_bias: float32 [1664], replicated, may hold values from -3 to 3
- vis_qkv: bfloat16 [3, 1664, 1664], P(None, None, 'tp'), may hold values from -2 to 2
- vis_out: bfloat16 [1664, 1664], P('tp'), may hold values from -0.15625 to 0.15625
- merge_weight: bfloat16 [4, 1664, 1024], P(None, 'tp'), may hold values from -0.078125 to 0.078125
- positions: int32 [4096], P('grp'), may hold values from 0 to 12287, as said below
- text: bfloat16 [8192, 1024], P('grp'), may hold values from -6 to 6
- dec_gain: float32 [1024], replicated, may hold values from 0.25 to 1.75
- dec_bias: float32 [1024], replicated, may hold values from -3 to 3
- dec_qkv: bfloat16 [3, 1024, 1024], P(None, None, 'tp'), may hold values from -2 to 2
Outputs:
- dec_attn: bfloat16 [12288, 1024], P('grp', 'tp')
Inputs may be any that keep to these rules, and one draw needn't show every extreme that they name: `patch_image`: each aligned run of four patches belongs to one image. Groups 2j and 2j+1 are partners: the last image of group 2j continues as the first image of group 2j+1; no other image is shared between groups. All positions are distinct; each group's block of 384 positions holds exactly 128 of them; the 128 merged rows of one group put at most 8 positions into any one group's block.
All inputs are finite; a program needn't handle non-finite values.
Results may differ from a plain program's by a relative error of at most 0.025.
Values may be sent and summed in bfloat16 or wider, within the bound.
No kernel may reach another device: no remote copies, remote signals or barrier semaphores. Data moves between devices by JAX's collectives and lax.ppermute only.
A program may use at most 128 MiB of HBM per device.

v0:
```python
import jax
import jax.numpy as jnp
from jax import lax
from jax.sharding import PartitionSpec as P

HD = 104
DH = 64
layer_eps = 1e-05


def swapped(value, axis, stride):
    return lax.ppermute(value, axis, [(i, i ^ 1 << stride) for i in range(lax.axis_size(axis))])


def normalize(values, gain, bias):
    mean = jnp.mean(values, axis=-1, keepdims=True)
    centred = values - mean
    spread = jnp.mean(centred * centred, axis=-1, keepdims=True)
    return centred * lax.rsqrt(spread + layer_eps) * gain + bias


def body(
    patches,
    patch_image,
    vis_gain,
    vis_bias,
    vis_qkv,
    vis_out,
    merge_weight,
    positions,
    text,
    dec_gain,
    dec_bias,
    dec_qkv,
):
    rows = patches.shape[0]
    heads = vis_qkv.shape[2] // HD
    patches_f = patches.astype(jnp.float32)
    normed = normalize(patches_f, vis_gain, vis_bias).astype(jnp.bfloat16)
    proj = jnp.einsum("pd,sde->spe", normed, vis_qkv, preferred_element_type=jnp.float32).astype(
        jnp.bfloat16
    )
    query = proj[0].reshape(rows, heads, HD)
    partner_kv, partner_ids = swapped((proj[1:], patch_image), "grp", 0)
    both_kv = jnp.concatenate([proj[1:], partner_kv], axis=1)
    both_ids = jnp.concatenate([patch_image, partner_ids], axis=0)
    keys = both_kv[0].reshape(2 * rows, heads, HD)
    values = both_kv[1].reshape(2 * rows, heads, HD)
    scores = jnp.einsum("phe,khe->hpk", query, keys, preferred_element_type=jnp.float32) * HD ** (
        -0.5
    )
    same = patch_image[:, None] == both_ids[None, :]
    top = jnp.max(jnp.where(same, scores, -1e30), axis=2, keepdims=True)
    expo = jnp.where(same, jnp.exp(scores - top), 0.0)
    weights = (expo / jnp.sum(expo, axis=2, keepdims=True)).astype(jnp.bfloat16)
    attended = jnp.einsum(
        "hpk,khe->phe", weights, values, preferred_element_type=jnp.float32
    ).astype(jnp.bfloat16)
    attended = attended.reshape(rows, heads * HD)
    width = patches.shape[1] // lax.axis_size("tp")
    mixed = lax.psum_scatter(
        lax.dot_general(
            vis_out, attended, (((0,), (1,)), ((), ())), preferred_element_type=jnp.float32
        ).astype(jnp.bfloat16),
        "tp",
        scatter_dimension=0,
        tiled=True,
    ).astype(jnp.float32)
    own_cols = lax.dynamic_slice_in_dim(patches_f, lax.axis_index("tp") * width, width, 1)
    visual = (mixed + own_cols.T).astype(jnp.bfloat16)
    windows = visual.reshape(width, rows // 4, 4)
    partial_rows = jnp.einsum(
        "cmk,kce->me", windows, merge_weight, preferred_element_type=jnp.float32
    )
    groups = lax.axis_size("grp")
    here = lax.axis_index("grp")
    merged_count = rows // 4
    text_count = text.shape[0]
    tok = text_count + merged_count
    cap = merged_count // min(groups, 16)
    target = positions // tok
    member = (target[:, None] == jnp.arange(groups, dtype=jnp.int32)[None, :]).astype(jnp.int32)
    rank = jnp.sum(jnp.cumsum(member, axis=0) * member, axis=1) - 1
    slot = target * cap + rank
    select = slot[None, :] == jnp.arange(groups * cap, dtype=jnp.int32)[:, None]
    select_bf = select.astype(jnp.bfloat16)
    bucket_pos = jnp.sum(jnp.where(select, positions[None, :] + 1, 0), axis=1) - 1
    merged = lax.psum(partial_rows.astype(jnp.bfloat16), "tp")
    packed = jnp.dot(select_bf, merged, preferred_element_type=jnp.float32).astype(jnp.bfloat16)
    got_rows, got_pos = (
        lax.all_to_all(packed, "grp", split_axis=0, concat_axis=0, tiled=True),
        lax.all_to_all(bucket_pos, "grp", split_axis=0, concat_axis=0, tiled=True),
    )
    local_pos = got_pos - here * tok
    place = jnp.arange(tok, dtype=jnp.int32)
    landing = (local_pos[None, :] == place[:, None]) & (got_pos[None, :] >= 0)
    image_here = jnp.any(landing, axis=1).astype(jnp.int32)
    text_index = place - (jnp.cumsum(image_here) - image_here)
    text_pick = (image_here[:, None] == 0) & (
        text_index[:, None] == jnp.arange(text_count, dtype=jnp.int32)[None, :]
    )
    prompt = jnp.dot(landing.astype(jnp.bfloat16), got_rows, preferred_element_type=jnp.float32)
    prompt = prompt + jnp.dot(
        text_pick.astype(jnp.bfloat16), text, preferred_element_type=jnp.float32
    )
    dnorm = normalize(prompt, dec_gain, dec_bias).astype(jnp.bfloat16)
    dproj = jnp.einsum("td,sde->ste", dnorm, dec_qkv, preferred_element_type=jnp.float32).astype(
        jnp.bfloat16
    )
    dheads = dec_qkv.shape[2] // DH
    dquery = dproj[0].reshape(tok, dheads, DH)
    query_pos = here * tok + place
    best = jnp.full((dheads, tok), -1e30, jnp.float32)
    key_rows = lax.all_gather(dproj[1], "grp", axis=0, tiled=True).reshape(-1, dheads, DH)
    value_rows = lax.all_gather(dproj[2], "grp", axis=0, tiled=True).reshape(-1, dheads, DH)
    key_pos = jnp.arange(key_rows.shape[0], dtype=jnp.int32)
    score = jnp.einsum(
        "the,rhe->htr", dquery, key_rows, preferred_element_type=jnp.float32
    ) * DH ** (-0.5)
    allowed = key_pos[None, :] <= query_pos[:, None]
    new_best = jnp.maximum(best, jnp.max(jnp.where(allowed[None], score, -1e30), axis=2))
    expo_d = jnp.where(allowed[None], jnp.exp(score - new_best[:, :, None]), 0.0)
    total = jnp.sum(expo_d, axis=2)
    acc = jnp.einsum(
        "htr,rhe->hte", expo_d.astype(jnp.bfloat16), value_rows, preferred_element_type=jnp.float32
    )
    best, total, acc = (new_best, total, acc)
    result = acc / total[:, :, None]
    return result.transpose(1, 0, 2).reshape(tok, dheads * DH).astype(jnp.bfloat16)


def solution(mesh):
    in_specs = (
        P("grp", None),
        P("grp"),
        P(),
        P(),
        P(None, None, "tp"),
        P("tp", None),
        P(None, "tp", None),
        P("grp"),
        P("grp", None),
        P(),
        P(),
        P(None, None, "tp"),
    )
    out_specs = P("grp", "tp")
    return jax.shard_map(body, mesh=mesh, in_specs=in_specs, out_specs=out_specs, check_vma=False)
```

profile of v0, /device:TPU:8, one launch (start us, length us, event | category | flops | bytes accessed | tf_op | source)
XLA Modules:
  0.0 415.6 jit_solution(2915710087922539153)
XLA Ops:
  6.5 0.0 copy-start
  6.5 0.0 reduce-scatter.4.cloned.1.call-start
  6.6 1.9 convert_reduce_fusion
  8.5 0.1 copy-done.1
  8.6 0.6 multiply_reduce_fusion
  9.2 0.0 copy-start.4
  9.2 1.0 fusion.6
  10.3 7.7 %collective-permute-start = (bf16[2,512,104]{1,2,0:T(8,128)(2,1)S(1)}, bf16[2,512,104]{1,2,0:T(8,128)(2,1)S(1)}, u32[]{:S(2)}, u32[]{:S(2)}) collective-permute-start(bf16[2,512,104]{1,2,0:T(8,128)(2,1)S(1)} %slice.38), channel_id=1, source_target_pairs={{0,16},{16,0},{32,48},{48,32},{64,80},{80,64},{96,112},{112,96},{1... | collective-permute-start | bytes 638984 | tf_op jit(solution)/shard_map/ppermute | solution.py:12
  18.1 1.9 collective-permute-start.1
  20.0 3.6 collective-permute-done.1
  23.6 0.0 collective-permute-done
  23.6 0.6 fusion.5
  24.2 1.4 copy-done.2
  25.5 0.7 fusion.13
  26.2 4.3 %fusion.4 = bf16[1664,512]{0,1:T(8,128)(2,1)} fusion(bf16[104,1664]{1,0:T(8,128)(2,1)S(1)} %copy-done.6, f32[512,1024]{1,0:T(8,128)} %copy-done.2, f32[512]{0:T(512)S(1)} %fusion.13, f32[512]{0:T(512)S(1)} %get-tuple-element.11, s32[1024]{0:T(1024)S(1)} %pad_add_fusion, s32[512]{0:T(512)S(1)} %copy-done.4, bf16[2,512,104]{1,2,0:T(8,128)(2,1)S(1)} %slice.38, ...), kind=kOutput, calls=%fused_computation.10 | convolution fusion | flops 290738176 | bytes 4583424 | tf_op jit(solution)/shard_map/dot_general | solution.py:62
  30.5 3.6 copy.17
  34.1 0.0 reduce-scatter.4.cloned.1.call-update
  34.1 0.0 all-reduce.2.cloned.1.call-start
  34.2 0.0 copy-start.11
  34.2 2.0 convert_element_type.82
  36.2 0.0 copy-done.11
  36.2 0.1 fusion.64
  36.3 0.2 reduce_window_sum.30
  36.4 0.2 select_reduce_fusion.2
  36.6 0.1 select_reduce_fusion.1
  36.8 59.7 %reduce-scatter.4.cloned.1.call-done = bf16[104,512]{1,0:T(8,128)(2,1)} async-done(((bf16[1664,512]{1,0:T(8,128)(2,1)}), bf16[104,512]{1,0:T(8,128)(2,1)}) %reduce-scatter.4.cloned.1.call-update) | async-done | bytes 106512
  96.5 1.0 copy.18
  97.5 1.2 fusion.49
  98.7 2.2 fusion.15
  100.9 0.0 all-reduce.2.cloned.1.call-update
  100.9 0.0 copy-start.3
  100.9 0.7 sub.80
  101.6 9.9 %all-to-all-start = ((s32[32,8,1]{1,2,0:T(1,128)}), s32[32,8,1]{1,2,0:T(1,128)S(1)}, u32[]{:S(2)}, u32[]{:S(2)}) async-start(s32[32,8,1]{1,2,0:T(1,128)} %bitcast), calls=%async_computation | async-start | bytes 32768 | tf_op jit(solution)/shard_map/all_to_all | solution.py:92
  111.5 102.0 %all-reduce.2.cloned.1.call-done = bf16[128,1024]{1,0:T(8,128)(2,1)} async-done(((bf16[128,1024]{1,0:T(8,128)(2,1)}), bf16[128,1024]{1,0:T(8,128)(2,1)}) %all-reduce.2.cloned.1.call-update) | async-done | bytes 262160 | tf_op jit(solution)/shard_map/psum | solution.py:88
  213.5 2.0 fusion.14
  215.5 0.0 all-to-all-done
  215.5 9.8 %all-to-all-start.1 = ((bf16[32,8,1024]{2,1,0:T(8,128)(2,1)}), bf16[32,8,1024]{2,1,0:T(8,128)(2,1)S(1)}, u32[]{:S(2)}, u32[]{:S(2)}) async-start(bf16[32,8,1024]{2,1,0:T(8,128)(2,1)} %fusion.14), calls=%async_computation.1 | async-start | bytes 1048576 | tf_op jit(solution)/shard_map/all_to_all | solution.py:91
  225.4 0.0 all-gather.5.cloned.1.call-start
  225.5 0.1 sub.83
  225.6 0.1 compare_reduce_fusion
  225.6 0.1 ge.16
  225.7 0.2 fusion.45
  225.9 0.3 reduce-window.9
  226.2 0.1 slice.33
  226.3 0.1 slice_reduce_fusion
  226.4 0.1 fusion.65
  226.5 16.5 %all-to-all-done.1 = bf16[32,8,1024]{2,1,0:T(8,128)(2,1)S(1)} async-done(((bf16[32,8,1024]{2,1,0:T(8,128)(2,1)}), bf16[32,8,1024]{2,1,0:T(8,128)(2,1)S(1)}, u32[]{:S(2)}, u32[]{:S(2)}) %all-to-all-start.1) | async-done | bytes 524320 | tf_op jit(solution)/shard_map/all_to_all | solution.py:91
  243.0 0.4 fusion.42
  243.4 0.0 copy-start.5
  243.4 0.0 copy-start.9
  243.4 0.0 copy-start.10
  243.4 0.5 fusion.75
  244.0 0.3 multiply_reduce_fusion.1
  244.3 0.1 copy-done.5
  244.4 0.5 fusion.37
  245.0 0.6 fusion.74
  245.6 0.0 all-gather.5.cloned.1.call-update
  245.7 0.2 all-gather.7.cloned.1.call-start
  245.9 0.3 all-gather.7.cloned.1.call-update
  246.3 71.2 %all-gather.5.cloned.1.call-done = bf16[1,12288,64]{1,2,0:T(8,128)(2,1)} async-done(((bf16[1,384,64]{1,2,0:T(8,128)(2,1)}), bf16[1,12288,64]{1,2,0:T(8,128)(2,1)}) %all-gather.5.cloned.1.call-update) | async-done | bytes 1572880 | tf_op jit(solution)/shard_map/all_gather | solution.py:114
  317.4 9.3 %select_reduce_fusion = (f32[384]{0:T(512)S(1)}, f32[384,12288]{1,0:T(8,128)}) fusion(s32[384]{0:T(512)S(1)} %iota_add_fusion, bf16[1,12288,64]{1,2,0:T(8,128)(2,1)} %all-gather.5.cloned.1.call-done, bf16[3,384,64]{1,2,0:T(8,128)(2,1)S(1)} %convert_bitcast_fusion.1), kind=kOutput, calls=%fused_computation.1 | convolution fusion | flops 622853760 | bytes 20499968 | tf_op jit(solution)/shard_map/the,rhe->htr/dot_general | solution.py:117
  326.7 11.1 %fusion = f32[384]{0:T(512)S(1)} fusion(f32[384,12288]{1,0:T(8,128)} %get-tuple-element.16, f32[384]{0:T(512)S(1)} %broadcast_maximum_fusion, s32[384]{0:T(512)S(1)} %iota_add_fusion), kind=kLoop, calls=%fused_computation.4 | loop fusion | flops 18873984 | bytes 18878976 | tf_op jit(solution)/shard_map/reduce_sum | solution.py:123
  337.8 60.2 %all-gather.7.cloned.1.call-done = bf16[1,12288,64]{1,2,0:T(8,128)(2,1)} async-done(((bf16[1,384,64]{1,2,0:T(8,128)(2,1)}), bf16[1,12288,64]{1,2,0:T(8,128)(2,1)}) %all-gather.7.cloned.1.call-update) | async-done | bytes 1572880 | tf_op jit(solution)/shard_map/all_gather | solution.py:115
  398.0 11.1 %fusion.22 = bf16[384,64]{0,1:T(8,128)(2,1)} fusion(bf16[1,12288,64]{1,2,0:T(8,128)(2,1)} %all-gather.7.cloned.1.call-done, f32[384,12288]{1,0:T(8,128)} %get-tuple-element.16, f32[384]{0:T(512)S(1)} %broadcast_maximum_fusion, s32[384]{0:T(512)S(1)} %iota_add_fusion, f32[384]{0:T(512)S(1)} %fusion), kind=kOutput, calls=%fused_computation.34 | convolution fusion | flops 622903296 | bytes 20500992 | tf_op jit(solution)/shard_map/htr,rhe->hte/dot_general | solution.py:124
  (29 shorter events, 0.3 us)
Async XLA Ops:
  6.5 2.6 copy-start
  6.5 2.1 copy-start.1
  6.5 2.7 copy-start.8
  6.5 2.7 copy-start.7
  6.5 89.9 %reduce-scatter.4.cloned.1.call-start = ((), (), s32[]{:S(2)}) async-start(), calls=%async_computation.6 | async-start | bytes 1810432
  9.2 8.9 %copy-start.4 = (s32[512]{0:T(512)S(1)}, s32[512]{0:T(512)}, u32[]{:S(2)}) copy-start(s32[512]{0:T(512)} %param.13) | copy-start | bytes 6148
  10.3 13.2 %collective-permute-start = (bf16[2,512,104]{1,2,0:T(8,128)(2,1)S(1)}, bf16[2,512,104]{1,2,0:T(8,128)(2,1)S(1)}, u32[]{:S(2)}, u32[]{:S(2)}) collective-permute-start(bf16[2,512,104]{1,2,0:T(8,128)(2,1)S(1)} %slice.38), channel_id=1, source_target_pairs={{0,16},{16,0},{32,48},{48,32},{64,80},{80,64},{96,112},{112,96},{1... | collective-permute-start | bytes 638984 | tf_op jit(solution)/shard_map/ppermute | solution.py:12
  18.1 5.5 %collective-permute-start.1 = (s32[512]{0:T(512)S(1)}, s32[512]{0:T(512)S(1)}, u32[]{:S(2)}, u32[]{:S(2)}) collective-permute-start(s32[512]{0:T(512)S(1)} %copy-done.4), channel_id=1, source_target_pairs={{0,16},{16,0},{32,48},{48,32},{64,80},{80,64},{96,112},{112,96},{1... | collective-permute-start | bytes 6152 | tf_op jit(solution)/shard_map/ppermute | solution.py:12
  23.6 2.6 copy-start.6
  24.2 1.4 copy-start.2
  34.1 179.3 %all-reduce.2.cloned.1.call-start = ((), (), s32[]{:S(2)}) async-start(), calls=%async_computation.3 | async-start | bytes 524288 | tf_op jit(solution)/shard_map/psum | solution.py:88
  34.2 2.0 copy-start.11
  100.9 142.5 %copy-start.3 = (bf16[256,1024]{1,0:T(8,128)(2,1)S(1)}, bf16[256,1024]{1,0:T(8,128)(2,1)}, u32[]{:S(2)}) copy-start(bf16[256,1024]{1,0:T(8,128)(2,1)} %param.20) | copy-start | bytes 1572868
  101.6 113.9 %all-to-all-start = ((s32[32,8,1]{1,2,0:T(1,128)}), s32[32,8,1]{1,2,0:T(1,128)S(1)}, u32[]{:S(2)}, u32[]{:S(2)}) async-start(s32[32,8,1]{1,2,0:T(1,128)} %bitcast), calls=%async_computation | async-start | bytes 32768 | tf_op jit(solution)/shard_map/all_to_all | solution.py:92
  215.5 27.5 %all-to-all-start.1 = ((bf16[32,8,1024]{2,1,0:T(8,128)(2,1)}), bf16[32,8,1024]{2,1,0:T(8,128)(2,1)S(1)}, u32[]{:S(2)}, u32[]{:S(2)}) async-start(bf16[32,8,1024]{2,1,0:T(8,128)(2,1)} %fusion.14), calls=%async_computation.1 | async-start | bytes 1048576 | tf_op jit(solution)/shard_map/all_to_all | solution.py:91
  225.4 92.1 %all-gather.5.cloned.1.call-start = ((), (), s32[]{:S(2)}) async-start(), calls=%async_computation.4 | async-start | bytes 1622016 | tf_op jit(solution)/shard_map/all_gather | solution.py:114
  243.4 1.0 copy-start.5
  243.4 1.0 copy-start.9
  243.4 1.0 copy-start.10
  245.7 152.3 %all-gather.7.cloned.1.call-start = ((), (), s32[]{:S(2)}) async-start(), calls=%async_computation.5 | async-start | bytes 1622016 | tf_op jit(solution)/shard_map/all_gather | solution.py:115
Sparse Core Ops, SparseCore 0:
  34.3 62.1 reduce-scatter.3
  101.0 112.4 all-reduce.1
  245.8 71.5 all-gather.4
  320.4 77.5 all-gather.6
where the time goes:
time: 416 us
  waiting for transfers between devices  313 us (75%)
  matrix products  32 us (8%)
  starting transfers between devices  29.7 us (7%)
  other arithmetic  19 us (5%)
  between operations  13.4 us (3%)
  local copies, waits for them, and re-layouts  8.01 us (2%)
    psum x1, waiting for transfers between devices, body(): merged = lax.psum(partial_rows.astype(jnp.bfloat16), 'tp')  102 us
    all_gather x1, waiting for transfers between devices, body(): lax.all_gather(dproj[1], 'grp', axis=0, tiled=True).reshape(-1, dheads, DH)  71.2 us
    all_gather x1, waiting for transfers between devices, body(): lax.all_gather(dproj[2], 'grp', axis=0, tiled=True).reshape(-1, dheads, DH)  60.2 us
    unnamed x5, waiting for transfers between devices  60.1 us
    all_to_all x1, waiting for transfers between devices, body(): lax.all_to_all(packed, 'grp', split_axis=0, concat_axis=0, tiled=True)  16.5 us
    dot_general x1, matrix products, body(): jnp.einsum('htr,rhe->hte', expo_d.astype(jnp.bfloat16), value_rows, prefe...  11.1 us
    reduce_sum x1, other arithmetic, body(): total = jnp.sum(expo_d, axis=2)  11.1 us
    all_to_all x1, starting transfers between devices, body(): lax.all_to_all(bucket_pos, 'grp', split_axis=0, concat_axis=0, tiled=True)  9.88 us
  transfers between devices with their start and end apart: 8, of which 6 were waited for; matrix products, arithmetic and copies ran while one was open for 6% of the time, Pallas kernels for 0%

commit v1 on v0

--- a/solution.py
+++ b/solution.py
@@ -111,7 +111,9 @@
     dquery = dproj[0].reshape(tok, dheads, DH)
     query_pos = here * tok + place
     best = jnp.full((dheads, tok), -1e30, jnp.float32)
-    key_rows = lax.all_gather(dproj[1], "grp", axis=0, tiled=True).reshape(-1, dheads, DH)
+    key_rows = jnp.concatenate(
+        lax.all_to_all(jnp.stack([dproj[1]] * lax.axis_size("grp")), "grp", 0, 0), axis=0
+    ).reshape(-1, dheads, DH)
     value_rows = lax.all_gather(dproj[2], "grp", axis=0, tiled=True).reshape(-1, dheads, DH)
     key_pos = jnp.arange(key_rows.shape[0], dtype=jnp.int32)
     score = jnp.einsum(

time: 416 us -> 354 us (0.85)
  waiting for transfers between devices: 313 us -> 245 us
  starting transfers between devices: 29.7 us -> 34.5 us
    all_gather x1 -> x0, waiting for transfers between devices: 71.2 us -> none  [body(): lax.all_gather(dproj[1], 'grp', axis=0, tiled=True).reshape(-1, dheads, DH)]
    all_to_all x0 -> x1, waiting for transfers between devices: none -> 39 us  [body(): lax.all_to_all(jnp.stack([dproj[1]] * lax.axis_size('grp')), 'grp', 0, 0)]
    all_gather x1, waiting for transfers between devices: 60.2 us -> 24.1 us  [body(): lax.all_gather(dproj[2], 'grp', axis=0, tiled=True).reshape(-1, dheads, DH)]
    all_to_all x0 -> x1, starting transfers between devices: none -> 4.86 us  [body(): lax.all_to_all(jnp.stack([dproj[1]] * lax.axis_size('grp')), 'grp', 0, 0)]
    unnamed x5 -> x4, waiting for transfers between devices: 60.1 us -> 60.2 us
  transfers between devices with their start and end apart: 8 -> 8, of which waited for: 6 -> 6; matrix products, arithmetic and copies ran while one was open for 6% -> 7% of each run, Pallas kernels for 0% -> 0%
where the time goes in v1:
time: 354 us; the launch traced here: 353 us
  waiting for transfers between devices  245 us (69%)
  starting transfers between devices  34.5 us (10%)
  matrix products  31 us (9%)
  other arithmetic  19 us (5%)
  between operations  13.4 us (4%)
  local copies, waits for them, and re-layouts  9.56 us (3%)
    psum x1, waiting for transfers between devices, body(): merged = lax.psum(partial_rows.astype(jnp.bfloat16), 'tp')  102 us
    unnamed x4, waiting for transfers between devices  60.2 us
    all_to_all x1, waiting for transfers between devices, body(): lax.all_to_all(jnp.stack([dproj[1]] * lax.axis_size('grp')), 'grp', 0, 0)  39 us
    all_gather x1, waiting for transfers between devices, body(): lax.all_gather(dproj[2], 'grp', axis=0, tiled=True).reshape(-1, dheads, DH)  24.1 us
    all_to_all x1, waiting for transfers between devices, body(): lax.all_to_all(packed, 'grp', split_axis=0, concat_axis=0, tiled=True)  16.6 us
    dot_general x1, matrix products, body(): jnp.einsum('htr,rhe->hte', expo_d.astype(jnp.bfloat16), value_rows, prefe...  11.1 us
    reduce_sum x1, other arithmetic, body(): total = jnp.sum(expo_d, axis=2)  11.1 us
    all_to_all x1, starting transfers between devices, body(): lax.all_to_all(bucket_pos, 'grp', split_axis=0, concat_axis=0, tiled=True)  9.88 us
  transfers between devices with their start and end apart: 8, of which 6 were waited for; matrix products, arithmetic and copies ran while one was open for 7% of the time, Pallas kernels for 0%

profile of v1, /device:TPU:8, one launch (start us, length us, event | category | flops | bytes accessed | tf_op | source)
XLA Modules:
  0.0 352.9 jit_solution(12014397949162417747)
XLA Ops:
  6.5 0.0 reduce-scatter.4.cloned.1.call-start
  6.6 1.9 convert_reduce_fusion
  8.5 0.1 copy-done.1
  8.6 0.6 multiply_reduce_fusion
  9.2 0.0 copy-start.4
  9.2 1.0 fusion.6
  10.3 7.7 %collective-permute-start = (bf16[2,512,104]{1,2,0:T(8,128)(2,1)S(1)}, bf16[2,512,104]{1,2,0:T(8,128)(2,1)S(1)}, u32[]{:S(2)}, u32[]{:S(2)}) collective-permute-start(bf16[2,512,104]{1,2,0:T(8,128)(2,1)S(1)} %slice.41), channel_id=1, source_target_pairs={{0,16},{16,0},{32,48},{48,32},{64,80},{80,64},{96,112},{112,96},{1... | collective-permute-start | bytes 638984 | tf_op jit(solution)/shard_map/ppermute | solution.py:12
  18.1 1.9 collective-permute-start.1
  20.0 3.6 %collective-permute-done.1 = s32[512]{0:T(512)S(1)} collective-permute-done((s32[512]{0:T(512)S(1)}, s32[512]{0:T(512)S(1)}, u32[]{:S(2)}, u32[]{:S(2)}) %collective-permute-start.1) | collective-permute-done | bytes 2080 | tf_op jit(solution)/shard_map/ppermute | solution.py:12
  23.6 0.0 collective-permute-done
  23.6 0.6 fusion.5
  24.2 1.4 copy-done.2
  25.5 0.7 fusion.12
  26.2 4.3 %fusion.4 = bf16[1664,512]{0,1:T(8,128)(2,1)} fusion(bf16[104,1664]{1,0:T(8,128)(2,1)S(1)} %copy-done.6, f32[512,1024]{1,0:T(8,128)} %copy-done.2, f32[512]{0:T(512)S(1)} %fusion.12, f32[512]{0:T(512)S(1)} %get-tuple-element.11, s32[1024]{0:T(1024)S(1)} %pad_add_fusion, s32[512]{0:T(512)S(1)} %copy-done.4, bf16[2,512,104]{1,2,0:T(8,128)(2,1)S(1)} %slice.41, ...), kind=kOutput, calls=%fused_computation.10 | convolution fusion | flops 290738176 | bytes 4583424 | tf_op jit(solution)/shard_map/dot_general | solution.py:62
  30.5 3.6 %copy.23 = bf16[1664,512]{1,0:T(8,128)(2,1)} copy(bf16[1664,512]{0,1:T(8,128)(2,1)} %fusion.4) | data formatting | bytes 3407872
  34.1 0.0 reduce-scatter.4.cloned.1.call-update
  34.1 0.0 all-reduce.2.cloned.1.call-start
  34.2 0.0 copy-start.11
  34.2 2.0 convert_element_type.82
  36.2 0.0 copy-done.11
  36.2 0.1 fusion.63
  36.3 0.2 reduce_window_sum.30
  36.4 0.2 select_reduce_fusion.2
  36.6 0.1 select_reduce_fusion.1
  36.8 59.7 %reduce-scatter.4.cloned.1.call-done = bf16[104,512]{1,0:T(8,128)(2,1)} async-done(((bf16[1664,512]{1,0:T(8,128)(2,1)}), bf16[104,512]{1,0:T(8,128)(2,1)}) %reduce-scatter.4.cloned.1.call-update) | async-done | bytes 106512
  96.5 1.0 copy.24
  97.5 1.2 fusion.48
  98.7 2.2 fusion.14
  100.9 0.0 all-reduce.2.cloned.1.call-update
  100.9 0.0 copy-start.3
  100.9 0.7 sub.80
  101.6 9.9 %all-to-all-start = ((s32[32,8,1]{1,2,0:T(1,128)}), s32[32,8,1]{1,2,0:T(1,128)S(1)}, u32[]{:S(2)}, u32[]{:S(2)}) async-start(s32[32,8,1]{1,2,0:T(1,128)} %bitcast), calls=%async_computation | async-start | bytes 32768 | tf_op jit(solution)/shard_map/all_to_all | solution.py:92
  111.5 102.0 %all-reduce.2.cloned.1.call-done = bf16[128,1024]{1,0:T(8,128)(2,1)} async-done(((bf16[128,1024]{1,0:T(8,128)(2,1)}), bf16[128,1024]{1,0:T(8,128)(2,1)}) %all-reduce.2.cloned.1.call-update) | async-done | bytes 262160 | tf_op jit(solution)/shard_map/psum | solution.py:88
  213.5 2.0 fusion.13
  215.5 0.0 all-to-all-done
  215.5 9.8 %all-to-all-start.1 = ((bf16[32,8,1024]{2,1,0:T(8,128)(2,1)}), bf16[32,8,1024]{2,1,0:T(8,128)(2,1)S(1)}, u32[]{:S(2)}, u32[]{:S(2)}) async-start(bf16[32,8,1024]{2,1,0:T(8,128)(2,1)} %fusion.13), calls=%async_computation.1 | async-start | bytes 1048576 | tf_op jit(solution)/shard_map/all_to_all | solution.py:91
  225.4 0.1 sub.83
  225.5 0.1 compare_reduce_fusion
  225.6 0.1 ge.16
  225.7 0.2 fusion.44
  225.8 0.3 reduce-window.9
  226.1 0.1 slice.35
  226.3 0.1 slice_reduce_fusion
  226.4 0.1 fusion.64
  226.5 16.6 %all-to-all-done.1 = bf16[32,8,1024]{2,1,0:T(8,128)(2,1)S(1)} async-done(((bf16[32,8,1024]{2,1,0:T(8,128)(2,1)}), bf16[32,8,1024]{2,1,0:T(8,128)(2,1)S(1)}, u32[]{:S(2)}, u32[]{:S(2)}) %all-to-all-start.1) | async-done | bytes 524320 | tf_op jit(solution)/shard_map/all_to_all | solution.py:91
  243.0 0.4 fusion.41
  243.4 0.0 copy-start.5
  243.4 0.0 copy-start.9
  243.4 0.0 copy-start.10
  243.4 0.5 fusion.73
  244.0 0.3 multiply_reduce_fusion.1
  244.3 0.1 copy-done.5
  244.4 0.5 fusion.36
  245.0 0.6 slice_bitcast_fusion.2
  245.6 1.4 stack.3
  247.0 4.9 %all-to-all-start.2 = ((bf16[32,384,64]{1,2,0:T(8,128)(2,1)}), bf16[32,384,64]{1,2,0:T(8,128)(2,1)S(1)}, u32[]{:S(2)}, u32[]{:S(2)}) async-start(bf16[32,384,64]{1,2,0:T(8,128)(2,1)} %stack.3), calls=%async_computation.2 | async-start | bytes 3145728 | tf_op jit(solution)/shard_map/all_to_all | solution.py:115
  251.9 0.2 all-gather.3.cloned.1.call-start
  252.1 0.5 all-gather.3.cloned.1.call-update
  252.6 39.0 %all-to-all-done.2 = bf16[32,384,64]{1,2,0:T(8,128)(2,1)S(1)} async-done(((bf16[32,384,64]{1,2,0:T(8,128)(2,1)}), bf16[32,384,64]{1,2,0:T(8,128)(2,1)S(1)}, u32[]{:S(2)}, u32[]{:S(2)}) %all-to-all-start.2) | async-done | bytes 1572896 | tf_op jit(solution)/shard_map/all_to_all | solution.py:115
  291.7 0.2 copy.25
  291.9 8.3 %select_reduce_fusion = (f32[384]{0:T(512)S(1)}, f32[384,12288]{1,0:T(8,128)}) fusion(s32[384]{0:T(512)S(1)} %iota_add_fusion, bf16[12288,64]{0,1:T(8,128)(2,1)S(1)} %bitcast.81, bf16[3,384,64]{1,2,0:T(8,128)(2,1)S(1)} %convert_bitcast_fusion.1), kind=kOutput, calls=%fused_computation.1 | convolution fusion | flops 622853760 | bytes 20499968 | tf_op jit(solution)/shard_map/the,rhe->htr/dot_general | solution.py:119
  300.2 11.1 %fusion = f32[384]{0:T(512)S(1)} fusion(f32[384,12288]{1,0:T(8,128)} %get-tuple-element.16, f32[384]{0:T(512)S(1)} %broadcast_maximum_fusion, s32[384]{0:T(512)S(1)} %iota_add_fusion), kind=kLoop, calls=%fused_computation.4 | loop fusion | flops 18873984 | bytes 18878976 | tf_op jit(solution)/shard_map/reduce_sum | solution.py:125
  311.2 24.1 %all-gather.3.cloned.1.call-done = bf16[1,12288,64]{1,2,0:T(8,128)(2,1)} async-done(((bf16[1,384,64]{1,2,0:T(8,128)(2,1)}), bf16[1,12288,64]{1,2,0:T(8,128)(2,1)}) %all-gather.3.cloned.1.call-update) | async-done | bytes 1572880 | tf_op jit(solution)/shard_map/all_gather | solution.py:117
  335.3 11.1 %fusion.21 = bf16[384,64]{0,1:T(8,128)(2,1)} fusion(bf16[1,12288,64]{1,2,0:T(8,128)(2,1)} %all-gather.3.cloned.1.call-done, f32[384,12288]{1,0:T(8,128)} %get-tuple-element.16, f32[384]{0:T(512)S(1)} %broadcast_maximum_fusion, s32[384]{0:T(512)S(1)} %iota_add_fusion, f32[384]{0:T(512)S(1)} %fusion), kind=kOutput, calls=%fused_computation.33 | convolution fusion | flops 622903296 | bytes 20500992 | tf_op jit(solution)/shard_map/htr,rhe->hte/dot_general | solution.py:126
  (30 shorter events, 0.3 us)
Async XLA Ops:
  6.5 2.6 copy-start
  6.5 2.1 copy-start.1
  6.5 2.7 copy-start.8
  6.5 2.7 copy-start.7
  6.5 89.9 %reduce-scatter.4.cloned.1.call-start = ((), (), s32[]{:S(2)}) async-start(), calls=%async_computation.6 | async-start | bytes 1810432
  9.2 8.9 %copy-start.4 = (s32[512]{0:T(512)S(1)}, s32[512]{0:T(512)}, u32[]{:S(2)}) copy-start(s32[512]{0:T(512)} %param.13) | copy-start | bytes 6148
  10.3 13.2 %collective-permute-start = (bf16[2,512,104]{1,2,0:T(8,128)(2,1)S(1)}, bf16[2,512,104]{1,2,0:T(8,128)(2,1)S(1)}, u32[]{:S(2)}, u32[]{:S(2)}) collective-permute-start(bf16[2,512,104]{1,2,0:T(8,128)(2,1)S(1)} %slice.41), channel_id=1, source_target_pairs={{0,16},{16,0},{32,48},{48,32},{64,80},{80,64},{96,112},{112,96},{1... | collective-permute-start | bytes 638984 | tf_op jit(solution)/shard_map/ppermute | solution.py:12
  18.1 5.5 %collective-permute-start.1 = (s32[512]{0:T(512)S(1)}, s32[512]{0:T(512)S(1)}, u32[]{:S(2)}, u32[]{:S(2)}) collective-permute-start(s32[512]{0:T(512)S(1)} %copy-done.4), channel_id=1, source_target_pairs={{0,16},{16,0},{32,48},{48,32},{64,80},{80,64},{96,112},{112,96},{1... | collective-permute-start | bytes 6152 | tf_op jit(solution)/shard_map/ppermute | solution.py:12
  23.6 2.6 copy-start.6
  24.2 1.4 copy-start.2
  34.1 179.3 %all-reduce.2.cloned.1.call-start = ((), (), s32[]{:S(2)}) async-start(), calls=%async_computation.4 | async-start | bytes 524288 | tf_op jit(solution)/shard_map/psum | solution.py:88
  34.2 2.0 copy-start.11
  100.9 142.5 %copy-start.3 = (bf16[256,1024]{1,0:T(8,128)(2,1)S(1)}, bf16[256,1024]{1,0:T(8,128)(2,1)}, u32[]{:S(2)}) copy-start(bf16[256,1024]{1,0:T(8,128)(2,1)} %param.20) | copy-start | bytes 1572868
  101.6 113.9 %all-to-all-start = ((s32[32,8,1]{1,2,0:T(1,128)}), s32[32,8,1]{1,2,0:T(1,128)S(1)}, u32[]{:S(2)}, u32[]{:S(2)}) async-start(s32[32,8,1]{1,2,0:T(1,128)} %bitcast), calls=%async_computation | async-start | bytes 32768 | tf_op jit(solution)/shard_map/all_to_all | solution.py:92
  215.5 27.5 %all-to-all-start.1 = ((bf16[32,8,1024]{2,1,0:T(8,128)(2,1)}), bf16[32,8,1024]{2,1,0:T(8,128)(2,1)S(1)}, u32[]{:S(2)}, u32[]{:S(2)}) async-start(bf16[32,8,1024]{2,1,0:T(8,128)(2,1)} %fusion.13), calls=%async_computation.1 | async-start | bytes 1048576 | tf_op jit(solution)/shard_map/all_to_all | solution.py:91
  243.4 1.0 copy-start.5
  243.4 1.0 copy-start.9
  243.4 1.0 copy-start.10
  247.0 44.7 %all-to-all-start.2 = ((bf16[32,384,64]{1,2,0:T(8,128)(2,1)}), bf16[32,384,64]{1,2,0:T(8,128)(2,1)S(1)}, u32[]{:S(2)}, u32[]{:S(2)}) async-start(bf16[32,384,64]{1,2,0:T(8,128)(2,1)} %stack.3), calls=%async_computation.2 | async-start | bytes 3145728 | tf_op jit(solution)/shard_map/all_to_all | solution.py:115
  251.9 83.4 %all-gather.3.cloned.1.call-start = ((), (), s32[]{:S(2)}) async-start(), calls=%async_computation.5 | async-start | bytes 1622016 | tf_op jit(solution)/shard_map/all_gather | solution.py:117
Sparse Core Ops, SparseCore 0:
  34.3 62.1 reduce-scatter.3
  101.0 112.4 all-reduce.1
  255.8 79.4 all-gather.2
